TPU v7x, 128 devices: a whole 4x4x4 slice. The times are simulated.
128 devices in a mesh: row: 32 (over y, z_lo, x), col: 4 (over z_hi, core).
Axes of the slice: x: 4, y: 4, z: 4 (z_hi: 2, z_lo: 2; z = z_hi * 2 + z_lo), core: 2. Of those that a mesh axis runs over, the one named last changes fastest.
Arguments:
- ratings: bfloat16 [4, 262144, 512], P(None, ('row', 'col'))
- tile_mask: int32 [4, 2048, 4], P(None, ('row', 'col')), may hold values from 0 to 1, as said below
- tile_counts: int32 [128], replicated, may hold values from 1 to 16, as said below
- users: float32 [131072, 128], P(('row', 'col')), may hold values from -2 to 2
- user_accum: float32 [131072, 128], P(('row', 'col')), may hold values from 0.05 to 0.5
- items: float32 [65536, 128], P(('row', 'col')), may hold values from -2 to 2
- item_accum: float32 [65536, 128], P(('row', 'col')), may hold values from 0.05 to 0.5
Outputs:
- users_out: float32 [131072, 128], P(('row', 'col'))
- user_accum_out: float32 [131072, 128], P(('row', 'col'))
- items_out: float32 [65536, 128], P(('row', 'col'))
- item_accum_out: float32 [65536, 128], P(('row', 'col'))
- losses: float32 [4], replicated
Inputs may be any that keep to these rules, and one draw needn't show every extreme that they name: Each group of 4 positions has tile_counts summing to 32, and exactly one position of each group, not always the same, owns 2 * 8 tiles. `tile_mask`: in each stratum, the first slot's first item tile of every position is 1.
All inputs are finite; a program needn't handle non-finite values.
Results may differ from a plain program's by a relative error of at most 0.0025.
Values sent between devices are 32-bit elements; how exact they have to be, the bound alone decides.
No kernel may reach another device: no remote copies, remote signals or barrier semaphores. Data moves between devices by JAX's collectives and lax.ppermute only.
A program may use at most 64 MiB of HBM per device.

v0:
```python
import jax
import jax.numpy as jnp
from jax import lax
from jax.sharding import PartitionSpec as P

TILE = 128
UT = 8
STEPS = 3
ridge_weight = 0.02
step_rate = 0.05


def passed_along(value, axis, steps):
    count = lax.axis_size(axis)
    pairs = [(source, (source + steps) % count) for source in range(count)]
    return lax.ppermute(value, axis, pairs)


def update(user_fac, user_acc, item_fac, item_acc, rating_block, live_tiles):
    tile_size = user_fac.shape[0] // live_tiles.shape[0]
    user_half = user_fac.astype(jnp.bfloat16)
    item_half = item_fac.astype(jnp.bfloat16)
    predicted = lax.dot_general(
        user_half, item_half, (((1,), (1,)), ((), ())), preferred_element_type=jnp.float32
    )
    residue = predicted - rating_block.astype(jnp.float32)
    masked = (
        residue.reshape(live_tiles.shape[0], tile_size, live_tiles.shape[1], tile_size)
        * live_tiles[:, None, :, None]
    ).reshape(residue.shape)
    sq_error = jnp.sum(masked * residue)
    err_half = masked.astype(jnp.bfloat16)
    grad_user = (
        jnp.dot(err_half, item_half, preferred_element_type=jnp.float32)
        * float(item_fac.shape[0]) ** (-0.5)
        + ridge_weight * user_fac
    )
    grad_item = (
        lax.dot_general(
            err_half, user_half, (((0,), (0,)), ((), ())), preferred_element_type=jnp.float32
        )
        * float(UT * TILE) ** (-0.5)
        + ridge_weight * item_fac
    )
    user_acc = user_acc + grad_user * grad_user
    item_acc = item_acc + grad_item * grad_item
    user_fac = user_fac - step_rate * grad_user * lax.rsqrt(user_acc)
    item_fac = item_fac - step_rate * grad_item * lax.rsqrt(item_acc)
    return (user_fac, user_acc, item_fac, item_acc, sq_error)


def on_device(ratings, tile_mask, tile_counts, users, user_accum, items, item_accum):
    strata_count = ratings.shape[0]
    slot_count = tile_mask.shape[1]
    tile_size = ratings.shape[1] // slot_count
    group_size = lax.axis_size("col")
    member = lax.axis_index("col")
    arrived_rows = users.shape[0]
    group_counts = lax.dynamic_slice_in_dim(
        tile_counts, lax.axis_index("row") * group_size, group_size
    )
    ranks = jnp.arange(group_size, dtype=jnp.int32)
    start_tile = jnp.sum(jnp.where(ranks < member, group_counts, 0))
    own_count = jnp.sum(jnp.where(ranks == member, group_counts, 0))
    valid = (jnp.arange(slot_count, dtype=jnp.int32) < own_count).astype(jnp.float32)
    whole_pair = lax.all_gather(jnp.stack([users, user_accum]), "col", axis=1, tiled=True)
    pad_rows = slot_count * tile_size
    ext_pair = jnp.concatenate([whole_pair, whole_pair[:, :pad_rows]], axis=1)
    user_pair = lax.dynamic_slice_in_dim(ext_pair, start_tile * tile_size, pad_rows, 1)
    user_fac = user_pair[0]
    user_acc = user_pair[1]
    held_pair = jnp.stack([items, item_accum])
    loss_list = []
    for stratum in range(strata_count):
        live_tiles = tile_mask[stratum].astype(jnp.float32) * valid[:, None]
        item_fac = held_pair[0]
        item_acc = held_pair[1]
        for inner in range(STEPS):
            user_fac, user_acc, item_fac, item_acc, sq_error = update(
                user_fac, user_acc, item_fac, item_acc, ratings[stratum], live_tiles
            )
            if inner == 0:
                observed = jnp.sum(live_tiles) * float(tile_size * tile_size)
                loss_list.append(jnp.stack([sq_error, observed]))
        held_pair = jnp.stack([item_fac, item_acc])
        if stratum + 1 < strata_count:
            held_pair = passed_along(held_pair, ("row", "col"), 1)
    loss_parts = lax.psum(jnp.stack(loss_list), ("row", "col"))
    losses = loss_parts[:, 0] / loss_parts[:, 1]
    row_valid = jnp.repeat(valid, tile_size)[None, :, None] > 0.5
    kept_pair = jnp.where(row_valid, jnp.stack([user_fac, user_acc]), 0.0)
    frame_rows = group_size * arrived_rows + pad_rows
    frame_pair = lax.dynamic_update_slice_in_dim(
        jnp.zeros((2, frame_rows, kept_pair.shape[2]), jnp.float32),
        kept_pair,
        start_tile * tile_size,
        1,
    )
    users_pair = lax.psum_scatter(
        frame_pair[:, : group_size * arrived_rows], "col", scatter_dimension=1, tiled=True
    )
    return (users_pair[0], users_pair[1], held_pair[0], held_pair[1], losses)


def solution(mesh):
    return jax.shard_map(
        on_device,
        mesh=mesh,
        in_specs=(
            P(None, ("row", "col"), None),
            P(None, ("row", "col"), None),
            P(),
            P(("row", "col"), None),
            P(("row", "col"), None),
            P(("row", "col"), None),
            P(("row", "col"), None),
        ),
        out_specs=(
            P(("row", "col"), None),
            P(("row", "col"), None),
            P(("row", "col"), None),
            P(("row", "col"), None),
            P(),
        ),
        check_vma=False,
    )
```

profile of v0, /device:TPU:1, one launch (start us, length us, event | category | flops | bytes accessed | tf_op | source)
XLA Modules:
  0.0 256.5 jit_solution(1015268047695154100)
XLA Ops:
  7.2 2.3 pad_maximum_fusion
  9.6 0.7 fusion.116
  11.0 0.7 compare_convert_fusion
  11.6 0.7 fusion.121
  12.4 39.6 %all-gather.2.cloned.1.call-done = f32[2,4096,128]{2,1,0:T(8,128)} async-done(((f32[2,1024,128]{2,1,0:T(8,128)}), f32[2,4096,128]{2,1,0:T(8,128)}) %all-gather.2.cloned.1.call-update) | async-done | bytes 4194320 | tf_op jit(solution)/shard_map/all_gather | solution.py:66
  51.9 1.9 slice.96
  53.8 2.2 fusion.32
  56.0 0.6 mul.537
  57.4 1.9 multiply_reduce_fusion.3
  59.3 0.7 multiply_subtract_fusion.10
  60.2 0.8 multiply_subtract_fusion.19
  61.0 0.7 fusion.1
  61.7 0.8 multiply_subtract_fusion.18
  62.5 1.7 multiply_subtract_fusion.9
  64.2 0.7 fusion.3
  64.9 0.8 subtract_bitcast_fusion.3
  65.7 0.8 pad_maximum_fusion.1
  66.6 2.6 %multiply_subtract_fusion.8 = (f32[2048,128]{1,0:T(8,128)S(1)}, f32[2048,128]{1,0:T(8,128)S(1)}) fusion(f32[2048,128]{1,0:T(8,128)S(1)} %get-tuple-element.57, f32[2048,128]{1,0:T(8,128)} %get-tuple-element.58, f32[2048,128]{1,0:T(8,128)} %copy-done.1, f32[2,2048,128]{2,1,0:T(8,128)} %copy-done, bf16[2048,512]{1,0:T(8,128)(2,1)S(1)} %fusion.3, ...), kind=kOutput, calls=%fused_computation.106 | convolution fusion | flops 271646720 | bytes 8650752 | tf_op jit(solution)/shard_map/dot_general | solution.py:34
  69.2 3.8 %collective-permute-done = f32[2,512,128]{2,1,0:T(8,128)} collective-permute-done((f32[2,512,128]{2,1,0:T(8,128)}, f32[2,512,128]{2,1,0:T(8,128)}, u32[]{:S(2)}, u32[]{:S(2)}) %collective-permute-start) | collective-permute-done | bytes 524320 | tf_op jit(solution)/shard_map/ppermute | solution.py:16
  73.0 0.6 mul.573
  73.6 3.7 %multiply_reduce_fusion.2 = (f32[]{:T(128)}, bf16[2048,512]{1,0:T(8,128)(2,1)S(1)}) fusion(f32[256,8,4,128]{3,2,1,0:T(4,128)S(1)} %bitcast.246, bf16[4,2048,512]{2,1,0:T(8,128)(2,1)} %param.7, f32[2,512,128]{2,1,0:T(8,128)} %collective-permute-done, f32[2048,128]{1,0:T(8,128)S(1)} %get-tuple-element.25), kind=kOutput, calls=%fused_computation.36 | convolution fusion | flops 274989056 | bytes 9568260 | tf_op jit(solution)/shard_map/dot_general | solution.py:23
  77.3 1.9 multiply_subtract_fusion.17
  79.3 1.7 multiply_subtract_fusion.7
  81.0 0.7 fusion.5
  81.7 1.7 multiply_subtract_fusion.6
  83.4 1.7 multiply_subtract_fusion.16
  85.1 0.7 fusion.7
  85.9 0.7 multiply_add_fusion.22
  86.6 1.0 subtract_bitcast_fusion.2
  87.7 0.8 pad_maximum_fusion.2
  88.5 4.0 %collective-permute-start.1 = (f32[2,512,128]{2,1,0:T(8,128)}, f32[2,512,128]{2,1,0:T(8,128)}, u32[]{:S(2)}, u32[]{:S(2)}) collective-permute-start(f32[2,512,128]{2,1,0:T(8,128)} %pad_maximum_fusion.2), channel_id=1, source_target_pairs={{0,1},{1,2},{2,3},{3,4},{4,5},{5,6},{6,7},{7,8},{8,9},{9,10},{10,1... | collective-permute-start | bytes 1572872 | tf_op jit(solution)/shard_map/ppermute | solution.py:16
  92.5 1.9 multiply_subtract_fusion.5
  94.5 4.4 %collective-permute-done.1 = f32[2,512,128]{2,1,0:T(8,128)} collective-permute-done((f32[2,512,128]{2,1,0:T(8,128)}, f32[2,512,128]{2,1,0:T(8,128)}, u32[]{:S(2)}, u32[]{:S(2)}) %collective-permute-start.1) | collective-permute-done | bytes 524320 | tf_op jit(solution)/shard_map/ppermute | solution.py:16
  99.5 3.7 %multiply_reduce_fusion.1 = (f32[]{:T(128)}, bf16[2048,512]{1,0:T(8,128)(2,1)S(1)}) fusion(f32[256,8,4,128]{3,2,1,0:T(4,128)S(1)} %bitcast.249, bf16[4,2048,512]{2,1,0:T(8,128)(2,1)} %param.7, f32[2,512,128]{2,1,0:T(8,128)} %collective-permute-done.1, f32[2048,128]{1,0:T(8,128)S(1)} %get-tuple-element.65), kind=kOutput, calls=%fused_computation.35 | convolution fusion | flops 274989056 | bytes 9568260 | tf_op jit(solution)/shard_map/dot_general | solution.py:23
  103.2 1.9 multiply_subtract_fusion.15
  105.2 1.7 multiply_subtract_fusion.4
  106.9 0.7 fusion.9
  107.8 1.8 multiply_subtract_fusion.3
  109.6 1.7 multiply_subtract_fusion.14
  111.3 0.7 fusion.11
  112.0 0.7 multiply_add_fusion.17
  112.8 1.0 subtract_bitcast_fusion.1
  113.8 0.8 pad_maximum_fusion.3
  114.6 4.0 %collective-permute-start.2 = (f32[2,512,128]{2,1,0:T(8,128)}, f32[2,512,128]{2,1,0:T(8,128)}, u32[]{:S(2)}, u32[]{:S(2)}) collective-permute-start(f32[2,512,128]{2,1,0:T(8,128)} %pad_maximum_fusion.3), channel_id=1, source_target_pairs={{0,1},{1,2},{2,3},{3,4},{4,5},{5,6},{6,7},{7,8},{8,9},{9,10},{10,1... | collective-permute-start | bytes 1572872 | tf_op jit(solution)/shard_map/ppermute | solution.py:16
  118.8 2.3 multiply_subtract_fusion.2
  121.1 7.4 %collective-permute-done.2 = f32[2,512,128]{2,1,0:T(8,128)} collective-permute-done((f32[2,512,128]{2,1,0:T(8,128)}, f32[2,512,128]{2,1,0:T(8,128)}, u32[]{:S(2)}, u32[]{:S(2)}) %collective-permute-start.2) | collective-permute-done | bytes 524320 | tf_op jit(solution)/shard_map/ppermute | solution.py:16
  128.5 0.6 mul.645
  129.1 3.7 %multiply_reduce_fusion = (f32[]{:T(128)}, bf16[2048,512]{1,0:T(8,128)(2,1)S(1)}) fusion(f32[256,8,4,128]{3,2,1,0:T(4,128)S(1)} %bitcast.252, bf16[4,2048,512]{2,1,0:T(8,128)(2,1)} %param.7, f32[2,512,128]{2,1,0:T(8,128)} %collective-permute-done.2, f32[2048,128]{1,0:T(8,128)S(1)} %get-tuple-element.19), kind=kOutput, calls=%fused_computation.34 | convolution fusion | flops 274989056 | bytes 9568260 | tf_op jit(solution)/shard_map/dot_general | solution.py:23
  132.8 1.9 multiply_subtract_fusion.13
  134.8 1.8 multiply_subtract_fusion.1
  136.6 0.7 fusion.13
  137.3 0.8 multiply_subtract_fusion
  138.0 2.4 multiply_subtract_fusion.12
  140.5 0.7 fusion.15
  141.2 0.7 subtract_bitcast_fusion
  142.8 2.2 slice.105
  147.6 0.7 maximum_bitcast_fusion
  148.3 0.7 maximum_bitcast_fusion.1
  149.0 0.6 maximum_bitcast_fusion.2
  149.6 0.7 maximum_bitcast_fusion.3
  150.4 93.7 %psum.7 = f32[4,2]{1,0:T(4,128)S(1)} all-reduce(f32[4,2]{1,0:T(4,128)S(1)} %pad_maximum_fusion.4), channel_id=1, replica_groups=mesh['row'=32,'col'=4] {'row','col'}, use_global_device_ids=true, to_apply=%region_11.12 | all-reduce | flops 8 | bytes 64 | tf_op jit(solution)/shard_map/psum | solution.py:88
  244.1 0.7 fusion.115
  244.8 2.6 %multiply_subtract_fusion.11 = (f32[512,128]{1,0:T(8,128)}, f32[512,128]{1,0:T(8,128)}) fusion(f32[512,128]{1,0:T(8,128)S(1)} %get-tuple-element.77, f32[512,128]{1,0:T(8,128)} %get-tuple-element.78, f32[512,128]{1,0:T(8,128)} %copy-done.4, f32[2,512,128]{2,1,0:T(8,128)} %collective-permute-done.2, bf16[2048,512]{1,0:T(8,128)(2,1)S(1)} %fusion.15, ...), kind=kOutput, calls=%fused_computation.127 | convolution fusion | flops 269484032 | bytes 4718592 | tf_op jit(solution)/shard_map/dot_general | solution.py:39
  247.4 2.2 slice_bitcast_fusion.2
  (53 shorter events, 3.2 us)
Async XLA Ops:
  7.2 2.4 copy-start.8
  7.2 4.4 %copy-start.7 = (s32[4,16,4]{1,2,0:T(4,128)S(1)}, s32[4,16,4]{1,2,0:T(4,128)}, u32[]{:S(2)}) copy-start(s32[4,16,4]{1,2,0:T(4,128)} %param.8) | copy-start | bytes 3076
  7.2 44.8 %all-gather.2.cloned.1.call-start = ((), (), s32[]{:S(2)}) async-start(), calls=%async_computation.1 | async-start | bytes 5242880 | tf_op jit(solution)/shard_map/all_gather | solution.py:66
  9.5 237.9 %reduce-scatter.2.cloned.1.call-start = ((), (), s32[]{:S(2)}) async-start(), calls=%async_computation.2 | async-start | bytes 5242880 | tf_op jit(solution)/shard_map/reduce_scatter | solution.py:99
  51.9 4.7 %slice-start = ((s8[8388608]{0:T(1024)(128)(4,1)}), s8[4194304]{0:T(1024)(128)(4,1)S(1)}, s32[]{:S(2)}) async-start(s8[8388608]{0:T(1024)(128)(4,1)} %bitcast.238), calls=%async_computation.3 | async-start | bytes 8388608
  53.8 3.1 %slice-start.1 = ((s8[8388608]{0:T(1024)(128)(4,1)}), s8[4194304]{0:T(1024)(128)(4,1)S(1)}, s32[]{:S(2)}) async-start(s8[8388608]{0:T(1024)(128)(4,1)} %bitcast.238), calls=%async_computation.4 | async-start | bytes 8388608
  56.0 6.5 %copy-start = (f32[2,2048,128]{2,1,0:T(8,128)}, f32[2,2048,128]{2,1,0:T(8,128)S(1)}, u32[]{:S(2)}) copy-start(f32[2,2048,128]{2,1,0:T(8,128)S(1)} %fusion.32) | copy-start | bytes 6291460
  56.0 1.4 copy-start.5
  59.3 0.9 copy-start.6
  60.2 2.3 copy-start.1
  66.5 6.4 %collective-permute-start = (f32[2,512,128]{2,1,0:T(8,128)}, f32[2,512,128]{2,1,0:T(8,128)}, u32[]{:S(2)}, u32[]{:S(2)}) collective-permute-start(f32[2,512,128]{2,1,0:T(8,128)} %pad_maximum_fusion.1), channel_id=1, source_target_pairs={{0,1},{1,2},{2,3},{3,4},{4,5},{5,6},{6,7},{7,8},{8,9},{9,10},{10,1... | collective-permute-start | bytes 1572872 | tf_op jit(solution)/shard_map/ppermute | solution.py:16
  73.6 7.4 %slice-start.2 = ((s8[8388608]{0:T(1024)(128)(4,1)}), s8[4194304]{0:T(1024)(128)(4,1)S(1)}, s32[]{:S(2)}) async-start(s8[8388608]{0:T(1024)(128)(4,1)} %bitcast.240), calls=%async_computation.5 | async-start | bytes 8388608
  77.3 3.6 %slice-start.3 = ((s8[8388608]{0:T(1024)(128)(4,1)}), s8[4194304]{0:T(1024)(128)(4,1)S(1)}, s32[]{:S(2)}) async-start(s8[8388608]{0:T(1024)(128)(4,1)} %bitcast.240), calls=%async_computation.6 | async-start | bytes 8388608
  88.5 10.4 %collective-permute-start.1 = (f32[2,512,128]{2,1,0:T(8,128)}, f32[2,512,128]{2,1,0:T(8,128)}, u32[]{:S(2)}, u32[]{:S(2)}) collective-permute-start(f32[2,512,128]{2,1,0:T(8,128)} %pad_maximum_fusion.2), channel_id=1, source_target_pairs={{0,1},{1,2},{2,3},{3,4},{4,5},{5,6},{6,7},{7,8},{8,9},{9,10},{10,1... | collective-permute-start | bytes 1572872 | tf_op jit(solution)/shard_map/ppermute | solution.py:16
  99.5 7.4 %slice-start.4 = ((s8[8388608]{0:T(1024)(128)(4,1)}), s8[4194304]{0:T(1024)(128)(4,1)S(1)}, s32[]{:S(2)}) async-start(s8[8388608]{0:T(1024)(128)(4,1)} %bitcast.242), calls=%async_computation.7 | async-start | bytes 8388608
  103.2 1.9 copy-start.2
  103.2 3.7 %slice-start.5 = ((s8[8388608]{0:T(1024)(128)(4,1)}), s8[4194304]{0:T(1024)(128)(4,1)S(1)}, s32[]{:S(2)}) async-start(s8[8388608]{0:T(1024)(128)(4,1)} %bitcast.242), calls=%async_computation.8 | async-start | bytes 8388608
  106.9 0.9 copy-start.3
  114.6 13.9 %collective-permute-start.2 = (f32[2,512,128]{2,1,0:T(8,128)}, f32[2,512,128]{2,1,0:T(8,128)}, u32[]{:S(2)}, u32[]{:S(2)}) collective-permute-start(f32[2,512,128]{2,1,0:T(8,128)} %pad_maximum_fusion.3), channel_id=1, source_target_pairs={{0,1},{1,2},{2,3},{3,4},{4,5},{5,6},{6,7},{7,8},{8,9},{9,10},{10,1... | collective-permute-start | bytes 1572872 | tf_op jit(solution)/shard_map/ppermute | solution.py:16
  129.1 7.4 %slice-start.6 = ((s8[8388608]{0:T(1024)(128)(4,1)}), s8[4194304]{0:T(1024)(128)(4,1)S(1)}, s32[]{:S(2)}) async-start(s8[8388608]{0:T(1024)(128)(4,1)} %bitcast.244), calls=%async_computation.9 | async-start | bytes 8388608
  132.8 3.7 %slice-start.7 = ((s8[8388608]{0:T(1024)(128)(4,1)}), s8[4194304]{0:T(1024)(128)(4,1)S(1)}, s32[]{:S(2)}) async-start(s8[8388608]{0:T(1024)(128)(4,1)} %bitcast.244), calls=%async_computation.10 | async-start | bytes 8388608
  134.7 3.3 %copy-start.4 = (f32[512,128]{1,0:T(8,128)}, f32[512,128]{1,0:T(8,128)S(1)}, u32[]{:S(2)}) copy-start(f32[512,128]{1,0:T(8,128)S(1)} %get-tuple-element.76) | copy-start | bytes 786436
Sparse Core Ops, SparseCore 0:
  9.7 42.2 all-gather.1
  145.1 56.8 reduce-scatter.1
where the time goes:
time: 257 us
  blocking collectives  93.7 us (36%)
  matrix products  56 us (22%)
  waiting for transfers between devices  55.2 us (21%)
  between operations  17.7 us (7%)
  other arithmetic  15 us (6%)
  local copies, waits for them, and re-layouts  10.8 us (4%)
  starting transfers between devices  8.05 us (3%)
    psum x1, blocking collectives, on_device(): loss_parts = lax.psum(jnp.stack(loss_list), ('row', 'col'))  93.7 us
    all_gather x1, waiting for transfers between devices, on_device(): lax.all_gather(jnp.stack([users, user_accum]), 'col', axis=1, tiled=True)  39.6 us
    dot_general x12, matrix products, update(): jnp.dot(err_half, item_half, preferred_element_type=jnp.float32)  19.3 us
    dot_general x12, matrix products, update(): lax.dot_general(user_half, item_half, (((1,), (1,)), ((), ())), preferred...  18.7 us
    dot_general x12, matrix products, update(): lax.dot_general(err_half, user_half, (((0,), (0,)), ((), ())), preferred_...  18.1 us
    ppermute x3, waiting for transfers between devices, passed_along(): return lax.ppermute(value, axis, pairs)  15.6 us
    ppermute x3, starting transfers between devices, passed_along(): return lax.ppermute(value, axis, pairs)  7.97 us
  transfers between devices with their start and end apart: 5, of which 4 were waited for; matrix products, arithmetic and copies ran while one was open for 6% of the time, Pallas kernels for 0%

commit v1 on v0

--- a/solution.py
+++ b/solution.py
@@ -85,7 +85,7 @@
         held_pair = jnp.stack([item_fac, item_acc])
         if stratum + 1 < strata_count:
             held_pair = passed_along(held_pair, ("row", "col"), 1)
-    loss_parts = lax.psum(jnp.stack(loss_list), ("row", "col"))
+    loss_parts = jnp.sum(lax.all_gather(jnp.stack(loss_list), ("row", "col")), axis=0)
     losses = loss_parts[:, 0] / loss_parts[:, 1]
     row_valid = jnp.repeat(valid, tile_size)[None, :, None] > 0.5
     kept_pair = jnp.where(row_valid, jnp.stack([user_fac, user_acc]), 0.0)

time: 257 us -> 346 us (1.35)
  blocking collectives: 93.7 us -> 183 us
    all_gather x0 -> x1, blocking collectives: none -> 183 us  [on_device(): lax.all_gather(jnp.stack(loss_list), ('row', 'col'))]
    psum x1 -> x0, blocking collectives: 93.7 us -> none  [on_device(): loss_parts = lax.psum(jnp.stack(loss_list), ('row', 'col'))]
  transfers between devices with their start and end apart: 5 -> 5, of which waited for: 4 -> 4; matrix products, arithmetic and copies ran while one was open for 6% -> 4% of each run, Pallas kernels for 0% -> 0%
where the time goes in v1:
time: 346 us
  blocking collectives  183 us (53%)
  matrix products  56 us (16%)
  waiting for transfers between devices  55.2 us (16%)
  between operations  17.6 us (5%)
  other arithmetic  15 us (4%)
  local copies, waits for them, and re-layouts  10.9 us (3%)
  starting transfers between devices  8.05 us (2%)
    all_gather x1, blocking collectives, on_device(): lax.all_gather(jnp.stack(loss_list), ('row', 'col'))  183 us
    all_gather x1, waiting for transfers between devices, on_device(): lax.all_gather(jnp.stack([users, user_accum]), 'col', axis=1, tiled=True)  39.6 us
    dot_general x12, matrix products, update(): jnp.dot(err_half, item_half, preferred_element_type=jnp.float32)  19.2 us
    dot_general x12, matrix products, update(): lax.dot_general(user_half, item_half, (((1,), (1,)), ((), ())), preferred...  18.7 us
    dot_general x12, matrix products, update(): lax.dot_general(err_half, user_half, (((0,), (0,)), ((), ())), preferred_...  18.1 us
    ppermute x3, waiting for transfers between devices, passed_along(): return lax.ppermute(value, axis, pairs)  15.6 us
    ppermute x3, starting transfers between devices, passed_along(): return lax.ppermute(value, axis, pairs)  7.97 us
  transfers between devices with their start and end apart: 5, of which 4 were waited for; matrix products, arithmetic and copies ran while one was open for 4% of the time, Pallas kernels for 0%

profile of v1, /device:TPU:1, one launch (start us, length us, event | category | flops | bytes accessed | tf_op | source)
XLA Modules:
  0.0 345.9 jit_solution(10753083027616618868)
XLA Ops:
  7.2 2.3 pad_maximum_fusion
  9.6 0.7 fusion.115
  11.0 0.7 compare_convert_fusion
  11.6 0.7 fusion.121
  12.4 39.6 %all-gather.4.cloned.1.call-done = f32[2,4096,128]{2,1,0:T(8,128)} async-done(((f32[2,1024,128]{2,1,0:T(8,128)}), f32[2,4096,128]{2,1,0:T(8,128)}) %all-gather.4.cloned.1.call-update) | async-done | bytes 4194320 | tf_op jit(solution)/shard_map/all_gather | solution.py:66
  51.9 1.9 slice.96
  53.8 2.2 fusion.32
  56.0 0.6 mul.537
  57.4 1.9 multiply_reduce_fusion.3
  59.3 0.7 multiply_subtract_fusion.10
  60.2 0.8 multiply_subtract_fusion.19
  61.0 0.7 fusion.1
  61.7 0.8 multiply_subtract_fusion.18
  62.5 1.7 multiply_subtract_fusion.9
  64.2 0.7 fusion.3
  64.9 0.8 subtract_bitcast_fusion.3
  65.7 0.8 pad_maximum_fusion.1
  66.6 2.6 multiply_subtract_fusion.8
  69.2 3.8 %collective-permute-done = f32[2,512,128]{2,1,0:T(8,128)} collective-permute-done((f32[2,512,128]{2,1,0:T(8,128)}, f32[2,512,128]{2,1,0:T(8,128)}, u32[]{:S(2)}, u32[]{:S(2)}) %collective-permute-start) | collective-permute-done | bytes 524320 | tf_op jit(solution)/shard_map/ppermute | solution.py:16
  72.9 0.6 mul.573
  73.6 3.7 %multiply_reduce_fusion.2 = (f32[]{:T(128)}, bf16[2048,512]{1,0:T(8,128)(2,1)S(1)}) fusion(f32[256,8,4,128]{3,2,1,0:T(4,128)S(1)} %bitcast.249, bf16[4,2048,512]{2,1,0:T(8,128)(2,1)} %param.7, f32[2,512,128]{2,1,0:T(8,128)} %collective-permute-done, f32[2048,128]{1,0:T(8,128)S(1)} %get-tuple-element.25), kind=kOutput, calls=%fused_computation.36 | convolution fusion | flops 274989056 | bytes 9568260 | tf_op jit(solution)/shard_map/dot_general | solution.py:23
  77.3 1.9 multiply_subtract_fusion.17
  79.2 1.7 multiply_subtract_fusion.7
  80.9 0.7 fusion.5
  81.7 1.7 multiply_subtract_fusion.6
  83.4 1.7 multiply_subtract_fusion.16
  85.1 0.7 fusion.7
  85.8 0.7 multiply_add_fusion.22
  86.6 1.0 subtract_bitcast_fusion.2
  87.6 0.8 pad_maximum_fusion.2
  88.4 4.0 %collective-permute-start.1 = (f32[2,512,128]{2,1,0:T(8,128)}, f32[2,512,128]{2,1,0:T(8,128)}, u32[]{:S(2)}, u32[]{:S(2)}) collective-permute-start(f32[2,512,128]{2,1,0:T(8,128)} %pad_maximum_fusion.2), channel_id=1, source_target_pairs={{0,1},{1,2},{2,3},{3,4},{4,5},{5,6},{6,7},{7,8},{8,9},{9,10},{10,1... | collective-permute-start | bytes 1572872 | tf_op jit(solution)/shard_map/ppermute | solution.py:16
  92.5 1.9 multiply_subtract_fusion.5
  94.4 4.4 %collective-permute-done.1 = f32[2,512,128]{2,1,0:T(8,128)} collective-permute-done((f32[2,512,128]{2,1,0:T(8,128)}, f32[2,512,128]{2,1,0:T(8,128)}, u32[]{:S(2)}, u32[]{:S(2)}) %collective-permute-start.1) | collective-permute-done | bytes 524320 | tf_op jit(solution)/shard_map/ppermute | solution.py:16
  98.9 0.6 mul.609
  99.5 3.7 %multiply_reduce_fusion.1 = (f32[]{:T(128)}, bf16[2048,512]{1,0:T(8,128)(2,1)S(1)}) fusion(f32[256,8,4,128]{3,2,1,0:T(4,128)S(1)} %bitcast.252, bf16[4,2048,512]{2,1,0:T(8,128)(2,1)} %param.7, f32[2,512,128]{2,1,0:T(8,128)} %collective-permute-done.1, f32[2048,128]{1,0:T(8,128)S(1)} %get-tuple-element.65), kind=kOutput, calls=%fused_computation.35 | convolution fusion | flops 274989056 | bytes 9568260 | tf_op jit(solution)/shard_map/dot_general | solution.py:23
  103.2 1.9 multiply_subtract_fusion.15
  105.1 1.7 multiply_subtract_fusion.4
  106.9 0.7 fusion.9
  107.8 1.7 multiply_subtract_fusion.3
  109.5 1.7 multiply_subtract_fusion.14
  111.3 0.7 fusion.11
  112.0 0.7 multiply_add_fusion.17
  112.7 1.0 subtract_bitcast_fusion.1
  113.8 0.8 pad_maximum_fusion.3
  114.6 4.0 %collective-permute-start.2 = (f32[2,512,128]{2,1,0:T(8,128)}, f32[2,512,128]{2,1,0:T(8,128)}, u32[]{:S(2)}, u32[]{:S(2)}) collective-permute-start(f32[2,512,128]{2,1,0:T(8,128)} %pad_maximum_fusion.3), channel_id=1, source_target_pairs={{0,1},{1,2},{2,3},{3,4},{4,5},{5,6},{6,7},{7,8},{8,9},{9,10},{10,1... | collective-permute-start | bytes 1572872 | tf_op jit(solution)/shard_map/ppermute | solution.py:16
  118.8 2.3 multiply_subtract_fusion.2
  121.0 7.5 %collective-permute-done.2 = f32[2,512,128]{2,1,0:T(8,128)} collective-permute-done((f32[2,512,128]{2,1,0:T(8,128)}, f32[2,512,128]{2,1,0:T(8,128)}, u32[]{:S(2)}, u32[]{:S(2)}) %collective-permute-start.2) | collective-permute-done | bytes 524320 | tf_op jit(solution)/shard_map/ppermute | solution.py:16
  128.5 0.6 mul.645
  129.1 3.7 %multiply_reduce_fusion = (f32[]{:T(128)}, bf16[2048,512]{1,0:T(8,128)(2,1)S(1)}) fusion(f32[256,8,4,128]{3,2,1,0:T(4,128)S(1)} %bitcast.255, bf16[4,2048,512]{2,1,0:T(8,128)(2,1)} %param.7, f32[2,512,128]{2,1,0:T(8,128)} %collective-permute-done.2, f32[2048,128]{1,0:T(8,128)S(1)} %get-tuple-element.19), kind=kOutput, calls=%fused_computation.34 | convolution fusion | flops 274989056 | bytes 9568260 | tf_op jit(solution)/shard_map/dot_general | solution.py:23
  132.8 1.9 multiply_subtract_fusion.13
  134.7 1.8 multiply_subtract_fusion.1
  136.5 0.7 fusion.13
  137.3 0.8 multiply_subtract_fusion
  138.0 2.4 multiply_subtract_fusion.12
  140.4 0.7 fusion.15
  141.2 0.7 subtract_bitcast_fusion
  142.8 2.2 slice.105
  147.5 0.7 maximum_bitcast_fusion
  148.2 0.7 maximum_bitcast_fusion.1
  148.9 0.7 maximum_bitcast_fusion.2
  149.6 0.7 maximum_bitcast_fusion.3
  150.4 183.1 %all-gather.1 = f32[128,4,2]{1,2,0:T(2,128)S(1)} all-gather(f32[1,4,2]{1,2,0:T(2,128)S(1)} %bitcast.263), channel_id=2, replica_groups=mesh['row'=32,'col'=4] {'row','col'}, dimensions={0}, use_global_device_ids=true | all-gather | bytes 4128 | tf_op jit(solution)/shard_map/all_gather | solution.py:88
  334.2 2.6 multiply_subtract_fusion.11
  336.8 2.2 slice_bitcast_fusion.2
  (55 shorter events, 3.4 us)
Async XLA Ops:
  7.2 2.4 copy-start.8
  7.2 4.4 %copy-start.7 = (s32[4,16,4]{1,2,0:T(4,128)S(1)}, s32[4,16,4]{1,2,0:T(4,128)}, u32[]{:S(2)}) copy-start(s32[4,16,4]{1,2,0:T(4,128)} %param.8) | copy-start | bytes 3076
  7.2 44.8 %all-gather.4.cloned.1.call-start = ((), (), s32[]{:S(2)}) async-start(), calls=%async_computation.1 | async-start | bytes 5242880 | tf_op jit(solution)/shard_map/all_gather | solution.py:66
  9.5 327.3 %reduce-scatter.2.cloned.1.call-start = ((), (), s32[]{:S(2)}) async-start(), calls=%async_computation.2 | async-start | bytes 5242880 | tf_op jit(solution)/shard_map/reduce_scatter | solution.py:99
  51.9 4.7 %slice-start = ((s8[8388608]{0:T(1024)(128)(4,1)}), s8[4194304]{0:T(1024)(128)(4,1)S(1)}, s32[]{:S(2)}) async-start(s8[8388608]{0:T(1024)(128)(4,1)} %bitcast.241), calls=%async_computation.3 | async-start | bytes 8388608
  53.8 3.1 slice-start.1
  56.0 6.5 %copy-start = (f32[2,2048,128]{2,1,0:T(8,128)}, f32[2,2048,128]{2,1,0:T(8,128)S(1)}, u32[]{:S(2)}) copy-start(f32[2,2048,128]{2,1,0:T(8,128)S(1)} %fusion.32) | copy-start | bytes 6291460
  56.0 1.4 copy-start.5
  59.3 0.9 copy-start.6
  60.2 2.3 copy-start.1
  66.5 6.4 %collective-permute-start = (f32[2,512,128]{2,1,0:T(8,128)}, f32[2,512,128]{2,1,0:T(8,128)}, u32[]{:S(2)}, u32[]{:S(2)}) collective-permute-start(f32[2,512,128]{2,1,0:T(8,128)} %pad_maximum_fusion.1), channel_id=1, source_target_pairs={{0,1},{1,2},{2,3},{3,4},{4,5},{5,6},{6,7},{7,8},{8,9},{9,10},{10,1... | collective-permute-start | bytes 1572872 | tf_op jit(solution)/shard_map/ppermute | solution.py:16
  73.5 7.4 %slice-start.2 = ((s8[8388608]{0:T(1024)(128)(4,1)}), s8[4194304]{0:T(1024)(128)(4,1)S(1)}, s32[]{:S(2)}) async-start(s8[8388608]{0:T(1024)(128)(4,1)} %bitcast.243), calls=%async_computation.5 | async-start | bytes 8388608
  77.3 3.6 %slice-start.3 = ((s8[8388608]{0:T(1024)(128)(4,1)}), s8[4194304]{0:T(1024)(128)(4,1)S(1)}, s32[]{:S(2)}) async-start(s8[8388608]{0:T(1024)(128)(4,1)} %bitcast.243), calls=%async_computation.6 | async-start | bytes 8388608
  88.4 10.4 %collective-permute-start.1 = (f32[2,512,128]{2,1,0:T(8,128)}, f32[2,512,128]{2,1,0:T(8,128)}, u32[]{:S(2)}, u32[]{:S(2)}) collective-permute-start(f32[2,512,128]{2,1,0:T(8,128)} %pad_maximum_fusion.2), channel_id=1, source_target_pairs={{0,1},{1,2},{2,3},{3,4},{4,5},{5,6},{6,7},{7,8},{8,9},{9,10},{10,1... | collective-permute-start | bytes 1572872 | tf_op jit(solution)/shard_map/ppermute | solution.py:16
  99.5 7.4 %slice-start.4 = ((s8[8388608]{0:T(1024)(128)(4,1)}), s8[4194304]{0:T(1024)(128)(4,1)S(1)}, s32[]{:S(2)}) async-start(s8[8388608]{0:T(1024)(128)(4,1)} %bitcast.245), calls=%async_computation.7 | async-start | bytes 8388608
  103.2 1.9 copy-start.2
  103.2 3.7 %slice-start.5 = ((s8[8388608]{0:T(1024)(128)(4,1)}), s8[4194304]{0:T(1024)(128)(4,1)S(1)}, s32[]{:S(2)}) async-start(s8[8388608]{0:T(1024)(128)(4,1)} %bitcast.245), calls=%async_computation.8 | async-start | bytes 8388608
  106.8 1.0 copy-start.3
  114.6 13.9 %collective-permute-start.2 = (f32[2,512,128]{2,1,0:T(8,128)}, f32[2,512,128]{2,1,0:T(8,128)}, u32[]{:S(2)}, u32[]{:S(2)}) collective-permute-start(f32[2,512,128]{2,1,0:T(8,128)} %pad_maximum_fusion.3), channel_id=1, source_target_pairs={{0,1},{1,2},{2,3},{3,4},{4,5},{5,6},{6,7},{7,8},{8,9},{9,10},{10,1... | collective-permute-start | bytes 1572872 | tf_op jit(solution)/shard_map/ppermute | solution.py:16
  129.1 7.4 %slice-start.6 = ((s8[8388608]{0:T(1024)(128)(4,1)}), s8[4194304]{0:T(1024)(128)(4,1)S(1)}, s32[]{:S(2)}) async-start(s8[8388608]{0:T(1024)(128)(4,1)} %bitcast.247), calls=%async_computation.9 | async-start | bytes 8388608
  132.8 3.7 %slice-start.7 = ((s8[8388608]{0:T(1024)(128)(4,1)}), s8[4194304]{0:T(1024)(128)(4,1)S(1)}, s32[]{:S(2)}) async-start(s8[8388608]{0:T(1024)(128)(4,1)} %bitcast.247), calls=%async_computation.10 | async-start | bytes 8388608
  134.7 3.3 copy-start.4
Sparse Core Ops, SparseCore 0:
  9.7 42.2 all-gather.3
  145.1 56.8 reduce-scatter.1
